TPU v7x, 128 devices: a whole 4x4x4 slice. The times are simulated.
128 devices in a mesh: row: 64 (over y, x, z_lo, core), col: 2 (over z_hi).
Axes of the slice: x: 4, y: 4, z: 4 (z_hi: 2, z_lo: 2; z = z_hi * 2 + z_lo), core: 2. Of those that a mesh axis runs over, the one named last changes fastest.
Arguments:
- dist_first: bfloat16 [32768, 32768], P('row', 'col'), may hold values from -0.34 to 0.34
- coupling: bfloat16 [32768, 256], P('row', 'col'), may hold values from 0.099609375 to 1
- dist_second: bfloat16 [256, 512], P(None, 'col'), may hold values from -12 to 12
- row_potential: float32 [32768], P('row'), may hold values from -150 to 120
- column_cost: float32 [512], P('col'), may hold values from -300 to 20
- column_mass: float32 [512], P('col'), may hold values from 0.5 to 2
Outputs:
- transport: bfloat16 [32768, 512], P('row', 'col')
- potential: float32 [512], P('col')
All inputs are finite; a program needn't handle non-finite values.
Results may differ from a plain program's by a relative error of at most 0.0051.
Values may be sent and summed in bfloat16 or wider, within the bound.
No kernel may reach another device: no remote copies, remote signals or barrier semaphores. Data moves between devices by JAX's collectives and lax.ppermute only.
A program may use at most 128 MiB of HBM per device.

v0:
```python
import jax
import jax.numpy as jnp
import numpy as np
from jax import lax
from jax.sharding import Mesh
from jax.sharding import PartitionSpec as P

N = 32768
AXES = ("yh", "yl", "x", "zl", "core", "zh")
ROWS = ("yh", "yl", "x", "zl", "core")
GATHER = ("yl", "x", "zl", "core")


def body(dist_first, coupling, dist_second, row_potential, column_cost, column_mass):
    zh = lax.axis_index("zh")
    yh = lax.axis_index("yh")
    blocks = coupling.shape[0]
    k_half = coupling.shape[1]
    q_half = dist_second.shape[1]
    coupling_x = lax.ppermute(coupling, "zh", [(0, 1), (1, 0)])
    second_x = lax.ppermute(dist_second, "zh", [(0, 1), (1, 0)])
    piece = jnp.concatenate([coupling, coupling_x], axis=1)
    into_other_half = [(0, 4), (2, 6), (5, 1), (7, 3)]
    moved = lax.ppermute(piece, ("yh", "yl", "zh"), into_other_half)
    piece = jnp.where(yh == zh, piece, moved)
    gathered = lax.all_gather(piece, GATHER, axis=0, tiled=True)
    second_full = jnp.concatenate([dist_second, second_x], axis=1)
    second_k = jnp.concatenate(
        [
            lax.dynamic_slice_in_dim(second_full, zh * k_half, k_half, axis=0),
            lax.dynamic_slice_in_dim(second_full, (1 - zh) * k_half, k_half, axis=0),
        ]
    )

    def partial_gradient(cols):
        product = jnp.dot(gathered, second_k[:, cols], preferred_element_type=jnp.float32).astype(
            jnp.bfloat16
        )
        return jnp.dot(dist_first, product, preferred_element_type=jnp.float32)

    other_part = partial_gradient(slice(q_half, 2 * q_half))
    arrived = lax.ppermute(other_part, "zh", [(0, 1), (1, 0)])
    own_part = partial_gradient(slice(0, q_half))
    own_part, arrived = lax.optimization_barrier((own_part, arrived))
    gradient = own_part + arrived
    scores = row_potential[:, None] + 2.0 * gradient - column_cost[None, :]
    local_high = jnp.max(scores, axis=0)
    local_sum = jnp.sum(jnp.exp(scores - local_high[None, :]), axis=0)
    stats = lax.all_gather(jnp.stack([local_high, local_sum]), ROWS, axis=0, tiled=False)
    highest = jnp.max(stats[:, 0], axis=0)
    column_sum = jnp.sum(stats[:, 1] * jnp.exp(stats[:, 0] - highest[None, :]), axis=0)
    weights = jnp.exp(scores - highest[None, :])
    potential = jnp.log(column_mass) - highest - jnp.log(column_sum)
    transport = (weights * (N * column_mass / column_sum)[None, :]).astype(jnp.bfloat16)
    return (transport, potential)


def solution(mesh):
    devices = np.asarray(mesh.devices).reshape(2, 2, 4, 2, 2, 2)
    fine = Mesh(devices, AXES)
    in_specs = (P(ROWS, "zh"), P(ROWS, "zh"), P(None, "zh"), P(ROWS), P("zh"), P("zh"))
    out_specs = (P(ROWS, "zh"), P("zh"))
    return jax.shard_map(body, mesh=fine, in_specs=in_specs, out_specs=out_specs, check_vma=False)
```

profile of v0, /device:TPU:1, one launch (start us, length us, event | category | flops | bytes accessed | tf_op | source)
XLA Modules:
  0.0 210.5 jit_solution(4188174330190762667)
XLA Ops:
  7.2 0.0 all-gather.4.cloned.1.call-start
  7.2 4.5 %collective-permute-start = (bf16[512,128]{1,0:T(8,128)(2,1)}, bf16[512,128]{1,0:T(8,128)(2,1)S(1)}, u32[]{:S(2)}, u32[]{:S(2)}) collective-permute-start(bf16[512,128]{1,0:T(8,128)(2,1)} %param.7), channel_id=1, source_target_pairs={{0,1},{1,0},{2,3},{3,2},{4,5},{5,4},{6,7},{7,6},{8,9},{9,8},{10,11... | collective-permute-start | bytes 393224 | tf_op jit(solution)/shard_map/ppermute | solution.py:20
  11.7 1.0 constant_dynamic-update-slice_fusion.1
  12.7 2.5 %collective-permute-done = bf16[512,128]{1,0:T(8,128)(2,1)S(1)} collective-permute-done((bf16[512,128]{1,0:T(8,128)(2,1)}, bf16[512,128]{1,0:T(8,128)(2,1)S(1)}, u32[]{:S(2)}, u32[]{:S(2)}) %collective-permute-start) | collective-permute-done | bytes 131104 | tf_op jit(solution)/shard_map/ppermute | solution.py:20
  15.2 4.8 %collective-permute-start.1 = (bf16[512,256]{1,0:T(8,128)(2,1)S(1)}, bf16[512,256]{1,0:T(8,128)(2,1)S(1)}, u32[]{:S(2)}, u32[]{:S(2)}) collective-permute-start(bf16[512,256]{1,0:T(8,128)(2,1)S(1)} %constant_dynamic-update-slice_fusion), channel_id=1, source_target_pairs={{0,64},{32,96},{65,1},{97,33},{2,66},{34,98},{67,3},{99,35},{4,68}... | collective-permute-start | bytes 786440 | tf_op jit(solution)/shard_map/ppermute | solution.py:24
  20.0 4.3 %collective-permute-done.1 = bf16[512,256]{1,0:T(8,128)(2,1)S(1)} collective-permute-done((bf16[512,256]{1,0:T(8,128)(2,1)S(1)}, bf16[512,256]{1,0:T(8,128)(2,1)S(1)}, u32[]{:S(2)}, u32[]{:S(2)}) %collective-permute-start.1) | collective-permute-done | bytes 262176 | tf_op jit(solution)/shard_map/ppermute | solution.py:24
  24.4 0.7 broadcast_select_fusion
  25.1 0.0 all-gather.4.cloned.1.call-update
  25.1 3.2 %collective-permute-start.2 = (bf16[256,256]{1,0:T(8,128)(2,1)}, bf16[256,256]{1,0:T(8,128)(2,1)S(1)}, u32[]{:S(2)}, u32[]{:S(2)}) collective-permute-start(bf16[256,256]{1,0:T(8,128)(2,1)} %param.8), channel_id=1, source_target_pairs={{0,1},{1,0},{2,3},{3,2},{4,5},{5,4},{6,7},{7,6},{8,9},{9,8},{10,11... | collective-permute-start | bytes 393224 | tf_op jit(solution)/shard_map/ppermute | solution.py:21
  28.3 0.9 constant_dynamic-update-slice_fusion.3
  29.3 1.6 collective-permute-done.2
  30.9 63.0 %all-gather.4.cloned.1.call-done = bf16[16384,256]{1,0:T(8,128)(2,1)} async-done(((bf16[512,256]{1,0:T(8,128)(2,1)}), bf16[16384,256]{1,0:T(8,128)(2,1)}) %all-gather.4.cloned.1.call-update) | async-done | bytes 8388624 | tf_op jit(solution)/shard_map/all_gather | solution.py:26
  93.9 11.7 %fusion.2 = f32[512,256]{0,1:T(8,128)S(1)} fusion(bf16[512,16384]{1,0:T(8,128)(2,1)} %param.6, bf16[16384,256]{1,0:T(8,128)(2,1)} %all-gather.4.cloned.1.call-done, bf16[128,512]{1,0:T(8,128)(2,1)S(1)} %get-tuple-element.12, bf16[128,512]{1,0:T(8,128)(2,1)S(1)} %get-tuple-element.13), kind=kOutput, calls=%fused_computation.4 | convolution fusion | flops 6446907392 | bytes 25952256 | tf_op jit(solution)/shard_map/dot_general | solution.py:39
  105.6 0.0 copy-start
  105.6 0.0 copy-start.1
  105.7 0.0 copy-start.2
  105.7 2.5 %collective-permute-start.3 = (f32[512,256]{0,1:T(8,128)S(1)}, f32[512,256]{0,1:T(8,128)S(1)}, u32[]{:S(2)}, u32[]{:S(2)}) collective-permute-start(f32[512,256]{0,1:T(8,128)S(1)} %fusion.2), channel_id=1, source_target_pairs={{0,1},{1,0},{2,3},{3,2},{4,5},{5,4},{6,7},{7,6},{8,9},{9,8},{10,11... | collective-permute-start | bytes 1572872 | tf_op jit(solution)/shard_map/ppermute | solution.py:42
  108.2 11.7 %fusion.3 = f32[512,256]{0,1:T(8,128)S(1)} fusion(bf16[512,16384]{1,0:T(8,128)(2,1)} %param.6, bf16[16384,256]{1,0:T(8,128)(2,1)} %all-gather.4.cloned.1.call-done, bf16[128,512]{1,0:T(8,128)(2,1)S(1)} %get-tuple-element.13, bf16[128,512]{1,0:T(8,128)(2,1)S(1)} %get-tuple-element.12), kind=kOutput, calls=%fused_computation.5 | convolution fusion | flops 6446907392 | bytes 25952256 | tf_op jit(solution)/shard_map/dot_general | solution.py:39
  119.9 0.6 collective-permute-done.3
  120.5 0.0 copy-done
  120.5 0.0 copy-done.1
  120.5 0.2 fusion.16
  120.7 0.2 exponential_reduce_fusion
  120.9 80.9 %all-gather.1 = f32[64,2,256]{2,1,0:T(2,128)S(1)} all-gather(f32[1,2,256]{2,1,0:T(2,128)S(1)} %maximum_bitcast_fusion), channel_id=2, replica_groups=mesh['yh'=2,'yl'=2,'x'=4,'zl'=2,'core'=2,'zh'=2] {'yh','yl','x','zl','co..., dimensions={0}, use_global_device_ids=true | all-gather | bytes 133120 | tf_op jit(solution)/shard_map/all_gather | solution.py:49
  201.9 0.1 slice_reduce_fusion
  202.1 0.0 copy-done.2
  202.1 0.6 log_subtract_fusion
  202.6 0.1 multiply_convert_fusion
  202.8 0.8 copy.11
  (5 shorter events, 0.1 us)
Async XLA Ops:
  7.2 86.8 %all-gather.4.cloned.1.call-start = ((), (), s32[]{:S(2)}) async-start(), calls=%async_computation | async-start | bytes 8650752 | tf_op jit(solution)/shard_map/all_gather | solution.py:26
  7.2 7.9 %collective-permute-start = (bf16[512,128]{1,0:T(8,128)(2,1)}, bf16[512,128]{1,0:T(8,128)(2,1)S(1)}, u32[]{:S(2)}, u32[]{:S(2)}) collective-permute-start(bf16[512,128]{1,0:T(8,128)(2,1)} %param.7), channel_id=1, source_target_pairs={{0,1},{1,0},{2,3},{3,2},{4,5},{5,4},{6,7},{7,6},{8,9},{9,8},{10,11... | collective-permute-start | bytes 393224 | tf_op jit(solution)/shard_map/ppermute | solution.py:20
  15.2 9.2 %collective-permute-start.1 = (bf16[512,256]{1,0:T(8,128)(2,1)S(1)}, bf16[512,256]{1,0:T(8,128)(2,1)S(1)}, u32[]{:S(2)}, u32[]{:S(2)}) collective-permute-start(bf16[512,256]{1,0:T(8,128)(2,1)S(1)} %constant_dynamic-update-slice_fusion), channel_id=1, source_target_pairs={{0,64},{32,96},{65,1},{97,33},{2,66},{34,98},{67,3},{99,35},{4,68}... | collective-permute-start | bytes 786440 | tf_op jit(solution)/shard_map/ppermute | solution.py:24
  25.1 5.8 %collective-permute-start.2 = (bf16[256,256]{1,0:T(8,128)(2,1)}, bf16[256,256]{1,0:T(8,128)(2,1)S(1)}, u32[]{:S(2)}, u32[]{:S(2)}) collective-permute-start(bf16[256,256]{1,0:T(8,128)(2,1)} %param.8), channel_id=1, source_target_pairs={{0,1},{1,0},{2,3},{3,2},{4,5},{5,4},{6,7},{7,6},{8,9},{9,8},{10,11... | collective-permute-start | bytes 393224 | tf_op jit(solution)/shard_map/ppermute | solution.py:21
  105.6 14.9 %copy-start = (f32[512]{0:T(512)S(1)}, f32[512]{0:T(512)}, u32[]{:S(2)}) copy-start(f32[512]{0:T(512)} %param.9) | copy-start | bytes 6148
  105.6 14.9 %copy-start.1 = (f32[256]{0:T(256)S(1)}, f32[256]{0:T(256)}, u32[]{:S(2)}) copy-start(f32[256]{0:T(256)} %param.10) | copy-start | bytes 3076
  105.7 96.4 %copy-start.2 = (f32[256]{0:T(256)S(1)}, f32[256]{0:T(256)}, u32[]{:S(2)}) copy-start(f32[256]{0:T(256)} %param.11) | copy-start | bytes 3076
  105.7 14.8 %collective-permute-start.3 = (f32[512,256]{0,1:T(8,128)S(1)}, f32[512,256]{0,1:T(8,128)S(1)}, u32[]{:S(2)}, u32[]{:S(2)}) collective-permute-start(f32[512,256]{0,1:T(8,128)S(1)} %fusion.2), channel_id=1, source_target_pairs={{0,1},{1,0},{2,3},{3,2},{4,5},{5,4},{6,7},{7,6},{8,9},{9,8},{10,11... | collective-permute-start | bytes 1572872 | tf_op jit(solution)/shard_map/ppermute | solution.py:42
Sparse Core Ops, SparseCore 0:
  25.2 68.6 all-gather.3
where the time goes:
time: 211 us; the launch traced here: 210 us
  blocking collectives  80.9 us (38%)
  waiting for transfers between devices  72.1 us (34%)
  matrix products  23.4 us (11%)
  starting transfers between devices  15.1 us (7%)
  between operations  14.1 us (7%)
  local copies, waits for them, and re-layouts  2.84 us (1%)
    all_gather x1, blocking collectives, body(): lax.all_gather(jnp.stack([local_high, local_sum]), ROWS, axis=0, tiled=Fa...  80.9 us
    all_gather x1, waiting for transfers between devices, body(): gathered = lax.all_gather(piece, GATHER, axis=0, tiled=True)  63 us
    dot_general x2, matrix products, partial_gradient(): return jnp.dot(dist_first, product, preferred_element_type=jnp.float32)  23.4 us
    ppermute x1, starting transfers between devices, body(): moved = lax.ppermute(piece, ('yh', 'yl', 'zh'), into_other_half)  4.83 us
    ppermute x1, starting transfers between devices, body(): coupling_x = lax.ppermute(coupling, 'zh', [(0, 1), (1, 0)])  4.51 us
    ppermute x1, waiting for transfers between devices, body(): moved = lax.ppermute(piece, ('yh', 'yl', 'zh'), into_other_half)  4.33 us
  transfers between devices with their start and end apart: 5, of which 5 were waited for; matrix products, arithmetic and copies ran while one was open for 6% of the time, Pallas kernels for 0%

commit v1 on v0

--- a/solution.py
+++ b/solution.py
@@ -1,3 +1,4 @@
+import functools
 import jax
 import jax.numpy as jnp
 import numpy as np
@@ -9,6 +10,15 @@
 AXES = ("yh", "yl", "x", "zl", "core", "zh")
 ROWS = ("yh", "yl", "x", "zl", "core")
 GATHER = ("yl", "x", "zl", "core")
+
+
+def _define_forms(u, axis_id):
+    return jnp.concatenate(
+        jax.lax.all_to_all(jnp.stack(jax.lax.axis_size(axis_id) * [u], 0), axis_id, 0, 0), 0
+    )
+
+
+compute_joints_in = functools.partial(_define_forms, axis_id=GATHER)
 
 
 def body(dist_first, coupling, dist_second, row_potential, column_cost, column_mass):
@@ -23,7 +33,7 @@
     into_other_half = [(0, 4), (2, 6), (5, 1), (7, 3)]
     moved = lax.ppermute(piece, ("yh", "yl", "zh"), into_other_half)
     piece = jnp.where(yh == zh, piece, moved)
-    gathered = lax.all_gather(piece, GATHER, axis=0, tiled=True)
+    gathered = compute_joints_in(piece)
     second_full = jnp.concatenate([dist_second, second_x], axis=1)
     second_k = jnp.concatenate(
         [

time: 211 us -> 251 us (1.19)
  waiting for transfers between devices: 72.1 us -> 107 us
  between operations: 14.1 us -> 0.77 us
  starting transfers between devices: 15.1 us -> 26.8 us
  blocking collectives: 80.9 us -> 85.2 us
  local copies, waits for them, and re-layouts: 2.84 us -> 6.08 us
    all_gather x1 -> x0, waiting for transfers between devices: 63 us -> none  [body(): gathered = lax.all_gather(piece, GATHER, axis=0, tiled=True)]
    ppermute x1, waiting for transfers between devices: 1.62 us -> 60.1 us  [body(): second_x = lax.ppermute(dist_second, 'zh', [(0, 1), (1, 0)])]
    all_to_all x0 -> x1, waiting for transfers between devices: none -> 39.8 us  [_define_forms(): jax.lax.all_to_all(jnp.stack(jax.lax.axis_size(axis_id) * [u], 0), axis_i...]
    all_to_all x0 -> x1, starting transfers between devices: none -> 7.31 us  [_define_forms(): jax.lax.all_to_all(jnp.stack(jax.lax.axis_size(axis_id) * [u], 0), axis_i...]
    all_gather x1, blocking collectives: 80.9 us -> 85.2 us  [body(): lax.all_gather(jnp.stack([local_high, local_sum]), ROWS, axis=0, tiled=Fa...]
    another operation x0 -> x1, local copies, waits for them, and re-layouts: none -> 4.17 us  [_define_forms(): jnp.stack(jax.lax.axis_size(axis_id) * [u], 0)]
    ppermute x1, starting transfers between devices: 2.49 us -> 5.08 us  [body(): arrived = lax.ppermute(other_part, 'zh', [(0, 1), (1, 0)])]
  transfers between devices with their start and end apart: 5 -> 5, of which waited for: 5 -> 4; matrix products, arithmetic and copies ran while one was open for 6% -> 5% of each run, Pallas kernels for 0% -> 0%
where the time goes in v1:
time: 251 us; the launch traced here: 250 us
  waiting for transfers between devices  107 us (43%)
  blocking collectives  85.2 us (34%)
  starting transfers between devices  26.8 us (11%)
  matrix products  23.4 us (9%)
  local copies, waits for them, and re-layouts  6.08 us (2%)
    all_gather x1, blocking collectives, body(): lax.all_gather(jnp.stack([local_high, local_sum]), ROWS, axis=0, tiled=Fa...  85.2 us
    ppermute x1, waiting for transfers between devices, body(): second_x = lax.ppermute(dist_second, 'zh', [(0, 1), (1, 0)])  60.1 us
    all_to_all x1, waiting for transfers between devices, _define_forms(): jax.lax.all_to_all(jnp.stack(jax.lax.axis_size(axis_id) * [u], 0), axis_i...  39.8 us
    dot_general x2, matrix products, partial_gradient(): return jnp.dot(dist_first, product, preferred_element_type=jnp.float32)  23.4 us
    all_to_all x1, starting transfers between devices, _define_forms(): jax.lax.all_to_all(jnp.stack(jax.lax.axis_size(axis_id) * [u], 0), axis_i...  7.31 us
    ppermute x1, starting transfers between devices, body(): arrived = lax.ppermute(other_part, 'zh', [(0, 1), (1, 0)])  5.08 us
    ppermute x1, starting transfers between devices, body(): second_x = lax.ppermute(dist_second, 'zh', [(0, 1), (1, 0)])  5.07 us
  transfers between devices with their start and end apart: 5, of which 4 were waited for; matrix products, arithmetic and copies ran while one was open for 5% of the time, Pallas kernels for 0%

profile of v1, /device:TPU:1, one launch (start us, length us, event | category | flops | bytes accessed | tf_op | source)
XLA Modules:
  0.0 250.4 jit_solution(10975865531687640288)
XLA Ops:
  0.6 4.5 %collective-permute-start = (bf16[512,128]{1,0:T(8,128)(2,1)}, bf16[512,128]{1,0:T(8,128)(2,1)S(1)}, u32[]{:S(2)}, u32[]{:S(2)}) collective-permute-start(bf16[512,128]{1,0:T(8,128)(2,1)} %param.7), channel_id=1, source_target_pairs={{0,1},{1,0},{2,3},{3,2},{4,5},{5,4},{6,7},{7,6},{8,9},{9,8},{10,11... | collective-permute-start | bytes 393224 | tf_op jit(solution)/shard_map/ppermute | solution.py:30
  5.1 1.0 constant_dynamic-update-slice_fusion.1
  6.1 2.5 collective-permute-done
  8.6 4.8 %collective-permute-start.1 = (bf16[512,256]{1,0:T(8,128)(2,1)S(1)}, bf16[512,256]{1,0:T(8,128)(2,1)S(1)}, u32[]{:S(2)}, u32[]{:S(2)}) collective-permute-start(bf16[512,256]{1,0:T(8,128)(2,1)S(1)} %constant_dynamic-update-slice_fusion), channel_id=1, source_target_pairs={{0,64},{32,96},{65,1},{97,33},{2,66},{34,98},{67,3},{99,35},{4,68}... | collective-permute-start | bytes 786440 | tf_op jit(solution)/shard_map/ppermute | solution.py:34
  13.5 4.3 %collective-permute-done.1 = bf16[512,256]{1,0:T(8,128)(2,1)S(1)} collective-permute-done((bf16[512,256]{1,0:T(8,128)(2,1)S(1)}, bf16[512,256]{1,0:T(8,128)(2,1)S(1)}, u32[]{:S(2)}, u32[]{:S(2)}) %collective-permute-start.1) | collective-permute-done | bytes 262176 | tf_op jit(solution)/shard_map/ppermute | solution.py:34
  17.8 4.2 %stack.8 = bf16[32,512,256]{2,1,0:T(8,128)(2,1)} broadcast(bf16[512,256]{1,0:T(8,128)(2,1)S(1)} %broadcast_select_fusion), dimensions={1,2} | broadcast | bytes 8650752 | tf_op jit(solution)/shard_map/stack | solution.py:17
  22.0 0.0 copy-start
  22.0 7.3 %all-to-all-start = ((bf16[32,512,256]{2,1,0:T(8,128)(2,1)}), bf16[32,512,256]{2,1,0:T(8,128)(2,1)}, u32[]{:S(2)}, u32[]{:S(2)}) async-start(bf16[32,512,256]{2,1,0:T(8,128)(2,1)} %stack.8), calls=%async_computation | async-start | bytes 16777216 | tf_op jit(solution)/shard_map/all_to_all | solution.py:17
  29.3 0.0 copy-done
  29.3 5.1 %collective-permute-start.2 = (bf16[256,256]{1,0:T(8,128)(2,1)S(1)}, bf16[256,256]{1,0:T(8,128)(2,1)S(1)}, u32[]{:S(2)}, u32[]{:S(2)}) collective-permute-start(bf16[256,256]{1,0:T(8,128)(2,1)S(1)} %copy-done), channel_id=1, source_target_pairs={{0,1},{1,0},{2,3},{3,2},{4,5},{5,4},{6,7},{7,6},{8,9},{9,8},{10,11... | collective-permute-start | bytes 393224 | tf_op jit(solution)/shard_map/ppermute | solution.py:31
  34.4 60.1 %collective-permute-done.2 = bf16[256,256]{1,0:T(8,128)(2,1)S(1)} collective-permute-done((bf16[256,256]{1,0:T(8,128)(2,1)S(1)}, bf16[256,256]{1,0:T(8,128)(2,1)S(1)}, u32[]{:S(2)}, u32[]{:S(2)}) %collective-permute-start.2) | collective-permute-done | bytes 131104 | tf_op jit(solution)/shard_map/ppermute | solution.py:31
  94.6 39.8 %all-to-all-done = bf16[32,512,256]{2,1,0:T(8,128)(2,1)} async-done(((bf16[32,512,256]{2,1,0:T(8,128)(2,1)}), bf16[32,512,256]{2,1,0:T(8,128)(2,1)}, u32[]{:S(2)}, u32[]{:S(2)}) %all-to-all-start) | async-done | bytes 8388640 | tf_op jit(solution)/shard_map/all_to_all | solution.py:17
  134.4 11.7 %fusion.2 = f32[512,256]{0,1:T(8,128)S(1)} fusion(bf16[512,16384]{1,0:T(8,128)(2,1)} %param.6, bf16[16384,256]{1,0:T(8,128)(2,1)} %bitcast, bf16[128,512]{1,0:T(8,128)(2,1)S(1)} %get-tuple-element.12, bf16[128,512]{1,0:T(8,128)(2,1)S(1)} %get-tuple-element.13), kind=kOutput, calls=%fused_computation.4 | convolution fusion | flops 6446907392 | bytes 25952256 | tf_op jit(solution)/shard_map/dot_general | solution.py:49
  146.1 0.0 copy-start.1
  146.1 0.0 copy-start.2
  146.1 0.0 copy-start.3
  146.1 5.1 %collective-permute-start.3 = (f32[512,256]{0,1:T(8,128)S(1)}, f32[512,256]{0,1:T(8,128)S(1)}, u32[]{:S(2)}, u32[]{:S(2)}) collective-permute-start(f32[512,256]{0,1:T(8,128)S(1)} %fusion.2), channel_id=1, source_target_pairs={{0,1},{1,0},{2,3},{3,2},{4,5},{5,4},{6,7},{7,6},{8,9},{9,8},{10,11... | collective-permute-start | bytes 1572872 | tf_op jit(solution)/shard_map/ppermute | solution.py:52
  151.2 11.7 %fusion.3 = f32[512,256]{0,1:T(8,128)S(1)} fusion(bf16[512,16384]{1,0:T(8,128)(2,1)} %param.6, bf16[16384,256]{1,0:T(8,128)(2,1)} %bitcast, bf16[128,512]{1,0:T(8,128)(2,1)S(1)} %get-tuple-element.13, bf16[128,512]{1,0:T(8,128)(2,1)S(1)} %get-tuple-element.12), kind=kOutput, calls=%fused_computation.5 | convolution fusion | flops 6446907392 | bytes 25952256 | tf_op jit(solution)/shard_map/dot_general | solution.py:49
  162.9 0.0 collective-permute-done.3
  162.9 0.0 copy-done.1
  162.9 0.0 copy-done.2
  163.0 0.2 fusion.16
  163.2 0.2 exponential_reduce_fusion
  163.4 85.2 %all-gather.1 = f32[64,2,256]{2,1,0:T(2,128)S(1)} all-gather(f32[1,2,256]{2,1,0:T(2,128)S(1)} %maximum_bitcast_fusion), channel_id=2, replica_groups=mesh['yh'=2,'yl'=2,'x'=4,'zl'=2,'core'=2,'zh'=2] {'yh','yl','x','zl','co..., dimensions={0}, use_global_device_ids=true | all-gather | bytes 133120 | tf_op jit(solution)/shard_map/all_gather | solution.py:59
  248.6 0.1 slice_reduce_fusion
  248.8 0.0 copy-done.3
  248.8 0.6 log_subtract_fusion
  249.4 0.1 multiply_convert_fusion
  249.6 0.8 copy.11
  (7 shorter events, 0.2 us)
Async XLA Ops:
  0.6 7.9 %collective-permute-start = (bf16[512,128]{1,0:T(8,128)(2,1)}, bf16[512,128]{1,0:T(8,128)(2,1)S(1)}, u32[]{:S(2)}, u32[]{:S(2)}) collective-permute-start(bf16[512,128]{1,0:T(8,128)(2,1)} %param.7), channel_id=1, source_target_pairs={{0,1},{1,0},{2,3},{3,2},{4,5},{5,4},{6,7},{7,6},{8,9},{9,8},{10,11... | collective-permute-start | bytes 393224 | tf_op jit(solution)/shard_map/ppermute | solution.py:30
  8.6 9.2 %collective-permute-start.1 = (bf16[512,256]{1,0:T(8,128)(2,1)S(1)}, bf16[512,256]{1,0:T(8,128)(2,1)S(1)}, u32[]{:S(2)}, u32[]{:S(2)}) collective-permute-start(bf16[512,256]{1,0:T(8,128)(2,1)S(1)} %constant_dynamic-update-slice_fusion), channel_id=1, source_target_pairs={{0,64},{32,96},{65,1},{97,33},{2,66},{34,98},{67,3},{99,35},{4,68}... | collective-permute-start | bytes 786440 | tf_op jit(solution)/shard_map/ppermute | solution.py:34
  22.0 7.3 %copy-start = (bf16[256,256]{1,0:T(8,128)(2,1)S(1)}, bf16[256,256]{1,0:T(8,128)(2,1)}, u32[]{:S(2)}) copy-start(bf16[256,256]{1,0:T(8,128)(2,1)} %param.8) | copy-start | bytes 393220
  22.0 112.4 %all-to-all-start = ((bf16[32,512,256]{2,1,0:T(8,128)(2,1)}), bf16[32,512,256]{2,1,0:T(8,128)(2,1)}, u32[]{:S(2)}, u32[]{:S(2)}) async-start(bf16[32,512,256]{2,1,0:T(8,128)(2,1)} %stack.8), calls=%async_computation | async-start | bytes 16777216 | tf_op jit(solution)/shard_map/all_to_all | solution.py:17
  29.3 65.2 %collective-permute-start.2 = (bf16[256,256]{1,0:T(8,128)(2,1)S(1)}, bf16[256,256]{1,0:T(8,128)(2,1)S(1)}, u32[]{:S(2)}, u32[]{:S(2)}) collective-permute-start(bf16[256,256]{1,0:T(8,128)(2,1)S(1)} %copy-done), channel_id=1, source_target_pairs={{0,1},{1,0},{2,3},{3,2},{4,5},{5,4},{6,7},{7,6},{8,9},{9,8},{10,11... | collective-permute-start | bytes 393224 | tf_op jit(solution)/shard_map/ppermute | solution.py:31
  146.1 16.8 %copy-start.1 = (f32[512]{0:T(512)S(1)}, f32[512]{0:T(512)}, u32[]{:S(2)}) copy-start(f32[512]{0:T(512)} %param.9) | copy-start | bytes 6148
  146.1 16.8 %copy-start.2 = (f32[256]{0:T(256)S(1)}, f32[256]{0:T(256)}, u32[]{:S(2)}) copy-start(f32[256]{0:T(256)} %param.10) | copy-start | bytes 3076
  146.1 102.7 %copy-start.3 = (f32[256]{0:T(256)S(1)}, f32[256]{0:T(256)}, u32[]{:S(2)}) copy-start(f32[256]{0:T(256)} %param.11) | copy-start | bytes 3076
  146.1 16.8 %collective-permute-start.3 = (f32[512,256]{0,1:T(8,128)S(1)}, f32[512,256]{0,1:T(8,128)S(1)}, u32[]{:S(2)}, u32[]{:S(2)}) collective-permute-start(f32[512,256]{0,1:T(8,128)S(1)} %fusion.2), channel_id=1, source_target_pairs={{0,1},{1,0},{2,3},{3,2},{4,5},{5,4},{6,7},{7,6},{8,9},{9,8},{10,11... | collective-permute-start | bytes 1572872 | tf_op jit(solution)/shard_map/ppermute | solution.py:52
